TPU v7x, 256 devices: a whole 4x4x8 slice. The times are simulated.
256 devices in a mesh: seq: 8 (over x, core), vocab: 32 (over z, y).
Axes of the slice: x: 4, y: 4, z: 8, core: 2. Of those that a mesh axis runs over, the one named last changes fastest.
Arguments:
- hidden: bfloat16 [2048, 4096], P('seq'), may hold values from -48 to 48
- head_weight: bfloat16 [4096, 65536], P('seq', 'vocab'), may hold values from -0.09375 to 0.09375
- queries: float32 [16, 65536], P(None, 'vocab'), may hold values from 0 to 1, as said below
- passage_lengths: int32 [32], replicated, may hold values from 1 to 192, 2048 in all
- pairing: int32 [32], replicated, may hold values from 0 to 15
- doc_freq: int32 [65536], P('vocab'), may hold values from 0 to 4194304
Outputs:
- grad_hidden: bfloat16 [2048, 4096], P('seq', 'vocab')
- losses: float32 [2], replicated
Inputs may be any that keep to these rules, and one draw needn't show every extreme that they name: `queries`: entries are nonnegative.
All inputs are finite; a program needn't handle non-finite values.
Results may differ from a plain program's by a relative error of at most 0.0039.
Values may be sent and summed in bfloat16 or wider, within the bound.
No kernel may reach another device: no remote copies, remote signals or barrier semaphores. Data moves between devices by JAX's collectives and lax.ppermute only.
A program may use at most 128 MiB of HBM per device.

v0:
```python
import jax
import jax.numpy as jnp
from jax import lax
from jax.sharding import Mesh, PartitionSpec as P

DOCS = 4194304
sharpness = 8.0
loss_scale = 16384.0
flops_weight = 32.0
highest = lax.Precision.HIGHEST
SEQ = ("sx", "sc")
VOC = ("vz", "vy")
GROUPS = 2


def butterfly(x, axes_sizes):
    for ax, n in axes_sizes:
        d = 1
        while d < n:
            x = jax.tree.map(lambda a: a + lax.ppermute(a, ax, [(i, i ^ d) for i in range(n)]), x)
            d *= 2
    return x


def halving_scatter(x, ax, n):
    me = lax.axis_index(ax)
    d = n // 2
    while d >= 1:
        h = x.shape[0] // 2
        bit = me // d % 2
        keep = lax.dynamic_slice_in_dim(x, bit * h, h, 0)
        send = lax.dynamic_slice_in_dim(x, (1 - bit) * h, h, 0)
        x = keep + lax.ppermute(send, ax, [(i, i ^ d) for i in range(n)])
        d //= 2
    return x


def softmax_terms(scores, pair_rows):
    onehot = (jnp.arange(scores.shape[0], dtype=jnp.int32)[:, None] == pair_rows[None, :]).astype(
        jnp.float32
    )
    peak_score = jnp.max(scores, axis=0)
    shifted = jnp.exp(scores - peak_score[None, :])
    denominator = jnp.sum(shifted, axis=0)
    log_total = peak_score + jnp.log(denominator)
    losses_each = log_total - jnp.sum(onehot * scores, axis=0)
    return (losses_each, shifted / denominator[None, :] - onehot)


def per_device(sizes, hidden, head_weight, queries, passage_lengths, pairing, doc_freq):
    n_sx, n_sc, n_vz, n_vy = sizes
    tok_rows = hidden.shape[0]
    vocab_cols = head_weight.shape[1]
    passages = passage_lengths.shape[0]
    vocab_total = vocab_cols * n_vz * n_vy
    finish = jnp.cumsum(passage_lengths)
    starts = finish - passage_lengths
    seq_index = lax.axis_index("sx") * n_sc + lax.axis_index("sc")
    position = seq_index * tok_rows + jnp.arange(tok_rows, dtype=jnp.int32)
    member = (
        (position[None, :] >= starts[:, None]) & (position[None, :] < finish[:, None])
    ).astype(jnp.float32)
    counts = passage_lengths.astype(jnp.float32)
    weights_df = jnp.log(1.0 + DOCS / (1.0 + doc_freq.astype(jnp.float32)))
    flops_grad = loss_scale * flops_weight * 2.0 / (vocab_total * passages)
    full_head = lax.all_gather(head_weight, SEQ, axis=0, tiled=True)
    logits = jnp.dot(hidden, full_head, preferred_element_type=jnp.float32)
    lifted = 1.0 + jax.nn.relu(logits)
    squared = lifted * lifted
    fourth = squared * squared
    powered = fourth * fourth
    local_sums = jnp.dot(member, powered, precision=highest)
    totals = butterfly(local_sums, [("sc", n_sc), ("sx", n_sx)])
    pooled = (jnp.log(totals) - jnp.log(counts)[:, None]) / sharpness
    col_mean = jnp.sum(pooled, axis=0) / passages
    flops_part = jnp.sum(weights_df * col_mean * col_mean) / vocab_total
    score_part = jnp.dot(queries, pooled.T, precision=highest)
    flops_row = jnp.where(jnp.arange(passages) == 0, flops_part, 0.0)[None, :]
    summed = butterfly(
        jnp.concatenate([score_part, flops_row], axis=0), [("vy", n_vy), ("vz", n_vz)]
    )
    scores, flops_value = (summed[:-1], summed[-1, 0])
    losses_each, probs = softmax_terms(scores, pairing)
    contrast = jnp.mean(losses_each)
    dscores = probs * (loss_scale / passages)
    dpooled = jnp.dot(dscores.T, queries, precision=highest) + flops_grad * weights_df * col_mean
    factor = dpooled / totals
    spread = lax.dot_general(member, factor, (((0,), (0,)), ((), ())), precision=highest)
    seventh = fourth * squared * lifted
    dlogits = jnp.where(logits > 0, spread * seventh, 0.0).astype(jnp.bfloat16)
    n_out = n_vz * n_vy
    width = full_head.shape[0] // n_out
    grouped = full_head.reshape(n_out, GROUPS, width // GROUPS, vocab_cols)
    pieces = []
    for g in range(GROUPS):
        rows = grouped[:, g].reshape(-1, vocab_cols)
        partial = lax.dot_general(
            rows, dlogits, (((1,), (1,)), ((), ())), preferred_element_type=jnp.float32
        )
        pieces.append(
            halving_scatter(
                lax.psum_scatter(partial, "vz", scatter_dimension=0, tiled=True), "vy", n_vy
            )
        )
    grad_cols = jnp.concatenate(pieces, axis=0)
    losses = jnp.stack([contrast, flops_value])
    return (grad_cols.T.astype(jnp.bfloat16), losses)


def solution(mesh):
    n_seq, n_voc = mesh.devices.shape
    n_sc = 2
    n_vy = 4
    sizes = (n_seq // n_sc, n_sc, n_voc // n_vy, n_vy)
    mesh4 = Mesh(mesh.devices.reshape(sizes), ("sx", "sc", "vz", "vy"))
    placed = (P(SEQ, None), P(SEQ, VOC), P(None, VOC), P(), P(), P(VOC))
    return jax.shard_map(
        lambda *a: per_device(sizes, *a),
        mesh=mesh4,
        in_specs=placed,
        out_specs=(P(SEQ, VOC), P()),
        check_vma=False,
    )
```

profile of v0, /device:TPU:10, one launch (start us, length us, event | category | flops | bytes accessed | tf_op | source)
XLA Modules:
  0.0 275.6 jit_solution(13790768649974117661)
XLA Ops:
  7.2 0.0 copy-start
  7.2 0.0 all-gather.2.cloned.1.call-start
  7.2 0.7 all-gather.2.cloned.1.call-update
  7.9 0.0 reduce-scatter.5.cloned.1.call-start
  8.0 0.0 copy-done.3
  8.0 0.1 copy.9
  8.1 0.1 reduce-window.8
  8.1 0.1 reduce
  8.3 91.5 %all-gather.2.cloned.1.call-done = bf16[4096,2048]{1,0:T(8,128)(2,1)} async-done(((bf16[512,2048]{1,0:T(8,128)(2,1)}), bf16[4096,2048]{1,0:T(8,128)(2,1)}) %all-gather.2.cloned.1.call-update) | async-done | bytes 16777232 | tf_op jit(solution)/shard_map/all_gather | solution.py:66
  99.8 8.1 %fusion.34 = f32[256,2048]{1,0:T(8,128)S(1)} fusion(bf16[256,4096]{1,0:T(8,128)(2,1)S(1)} %copy-done, bf16[4096,2048]{1,0:T(8,128)(2,1)} %all-gather.2.cloned.1.call-done), kind=kOutput, calls=%fused_computation.66 | convolution fusion | flops 4294967296 | bytes 20971520 | tf_op jit(solution)/shard_map/dot_general | solution.py:67
  107.9 0.0 copy-start.2
  108.0 0.0 copy-start.1
  108.0 1.2 fusion.3
  109.2 0.3 collective-permute-start
  109.5 1.3 collective-permute-done
  110.8 1.0 collective-permute-start.1
  111.8 7.6 %collective-permute-done.1 = f32[32,2048]{1,0:T(8,128)S(1)} collective-permute-done((f32[32,2048]{1,0:T(8,128)S(1)}, f32[32,2048]{1,0:T(8,128)S(1)}, u32[]{:S(2)}, u32[]{:S(2)}) %collective-permute-start.1) | collective-permute-done | bytes 262176 | tf_op jit(solution)/shard_map/ppermute | solution.py:20
  119.4 1.2 collective-permute-start.2
  120.7 7.9 %collective-permute-done.2 = f32[32,2048]{1,0:T(8,128)S(1)} collective-permute-done((f32[32,2048]{1,0:T(8,128)S(1)}, f32[32,2048]{1,0:T(8,128)S(1)}, u32[]{:S(2)}, u32[]{:S(2)}) %collective-permute-start.2) | collective-permute-done | bytes 262176 | tf_op jit(solution)/shard_map/ppermute | solution.py:20
  128.6 0.1 fusion.8
  128.8 0.6 fusion.17
  130.0 0.4 convolution_bitcast_fusion.2
  130.4 0.1 pad_maximum_fusion
  130.5 0.6 collective-permute-start.3
  131.1 3.2 %collective-permute-done.3 = f32[17,32]{1,0:T(8,128)S(1)} collective-permute-done((f32[17,32]{1,0:T(8,128)S(1)}, f32[17,32]{1,0:T(8,128)S(1)}, u32[]{:S(2)}, u32[]{:S(2)}) %collective-permute-start.3) | collective-permute-done | bytes 2208 | tf_op jit(solution)/shard_map/ppermute | solution.py:20
  134.3 2.1 collective-permute-start.4
  136.4 3.1 %collective-permute-done.4 = f32[17,32]{1,0:T(8,128)S(1)} collective-permute-done((f32[17,32]{1,0:T(8,128)S(1)}, f32[17,32]{1,0:T(8,128)S(1)}, u32[]{:S(2)}, u32[]{:S(2)}) %collective-permute-start.4) | collective-permute-done | bytes 2208 | tf_op jit(solution)/shard_map/ppermute | solution.py:20
  139.5 1.6 collective-permute-start.5
  141.0 2.1 collective-permute-done.5
  143.2 2.5 collective-permute-start.6
  145.7 2.1 collective-permute-done.6
  147.8 5.8 %collective-permute-start.7 = (f32[17,32]{1,0:T(8,128)S(1)}, f32[17,32]{1,0:T(8,128)S(1)}, u32[]{:S(2)}, u32[]{:S(2)}) collective-permute-start(f32[17,32]{1,0:T(8,128)S(1)} %add.116), channel_id=1, source_target_pairs={{0,16},{4,20},{8,24},{12,28},{16,0},{20,4},{24,8},{28,12},{1,17},{... | collective-permute-start | bytes 6536 | tf_op jit(solution)/shard_map/ppermute | solution.py:20
  153.5 9.9 %fusion.33 = (bf16[32,1,64,2048]{3,2,1,0:T(8,128)(2,1)}, bf16[32,1,64,2048]{3,2,1,0:T(8,128)(2,1)S(1)}) fusion(bf16[32,2,64,2048]{3,2,1,0:T(8,128)(2,1)} %bitcast.23), kind=kLoop, calls=%fused_computation.65 | loop fusion | bytes 33554432 | tf_op jit(solution)/shard_map/slice | solution.py:96
  163.4 0.0 collective-permute-done.7
  163.5 0.4 fusion.2
  163.9 1.6 fusion.1
  165.6 1.0 copy-done.7
  166.5 3.7 %convolution_bitcast_fusion = f32[2048,256]{0,1:T(8,128)} fusion(bf16[256,2048]{1,0:T(8,128)(2,1)S(1)} %fusion.1, bf16[2048,2048]{1,0:T(8,128)(2,1)S(1)} %bitcast.25), kind=kOutput, calls=%fused_computation.2 | convolution fusion | flops 2147483648 | bytes 11534336 | tf_op jit(solution)/shard_map/dot_general | solution.py:97
  170.2 0.0 reduce-scatter.5.cloned.1.call-update
  170.2 0.0 reduce-scatter.3.cloned.1.call-start
  170.3 7.4 %convolution_bitcast_fusion.1 = f32[2048,256]{0,1:T(8,128)} fusion(bf16[256,2048]{1,0:T(8,128)(2,1)} %copy-done.7, bf16[2048,2048]{1,0:T(8,128)(2,1)} %bitcast.24), kind=kOutput, calls=%fused_computation.3 | convolution fusion | flops 2147483648 | bytes 11534336 | tf_op jit(solution)/shard_map/dot_general | solution.py:97
  177.7 0.0 reduce-scatter.3.cloned.1.call-update
  177.8 0.5 slice.19
  178.3 0.6 subtract_reduce_fusion
  179.5 29.7 %reduce-scatter.5.cloned.1.call-done = f32[256,256]{0,1:T(8,128)} async-done(((f32[2048,256]{0,1:T(8,128)}), f32[256,256]{0,1:T(8,128)}) %reduce-scatter.5.cloned.1.call-update) | async-done | bytes 262160 | tf_op jit(solution)/shard_map/reduce_scatter | solution.py:102
  209.3 0.9 constant_dynamic-slice_fusion.1
  210.2 2.2 collective-permute-start.10
  212.4 1.2 pad_maximum_fusion.1
  213.6 39.7 %reduce-scatter.3.cloned.1.call-done = f32[256,256]{0,1:T(8,128)} async-done(((f32[2048,256]{0,1:T(8,128)}), f32[256,256]{0,1:T(8,128)}) %reduce-scatter.3.cloned.1.call-update) | async-done | bytes 262160 | tf_op jit(solution)/shard_map/reduce_scatter | solution.py:102
  253.3 0.9 constant_dynamic-slice_fusion.3
  254.2 1.9 collective-permute-start.8
  256.1 0.0 collective-permute-done.10
  256.1 0.9 dynamic-slice_add_fusion
  257.0 0.1 constant_dynamic-slice_fusion
  257.1 1.8 collective-permute-start.11
  259.0 3.1 %collective-permute-done.8 = f32[128,256]{0,1:T(8,128)S(1)} collective-permute-done((f32[128,256]{0,1:T(8,128)S(1)}, f32[128,256]{0,1:T(8,128)S(1)}, u32[]{:S(2)}, u32[]{:S(2)}) %collective-permute-start.8) | collective-permute-done | bytes 131104 | tf_op jit(solution)/shard_map/ppermute | solution.py:33
  262.1 0.9 dynamic-slice_add_fusion.1
  263.1 0.1 constant_dynamic-slice_fusion.2
  263.2 0.1 collective-permute-start.9
  263.3 0.0 collective-permute-done.11
  263.3 0.1 add_convert_fusion
  263.4 4.8 %collective-permute-done.9 = f32[64,256]{0,1:T(8,128)S(1)} collective-permute-done((f32[64,256]{0,1:T(8,128)S(1)}, f32[64,256]{0,1:T(8,128)S(1)}, u32[]{:S(2)}, u32[]{:S(2)}) %collective-permute-start.9) | collective-permute-done | bytes 65568 | tf_op jit(solution)/shard_map/ppermute | solution.py:33
  268.2 0.1 add_convert_fusion.1
  268.3 0.7 maximum_bitcast_fusion
  (24 shorter events, 0.2 us)
Async XLA Ops:
  7.2 92.6 %copy-start = (bf16[256,4096]{1,0:T(8,128)(2,1)S(1)}, bf16[256,4096]{1,0:T(8,128)(2,1)}, u32[]{:S(2)}) copy-start(bf16[256,4096]{1,0:T(8,128)(2,1)} %param.6) | copy-start | bytes 6291460
  7.2 0.8 copy-start.3
  7.2 92.6 %all-gather.2.cloned.1.call-start = ((), (), s32[]{:S(2)}) async-start(), calls=%async_computation.2 | async-start | bytes 18874368 | tf_op jit(solution)/shard_map/all_gather | solution.py:66
  7.9 201.4 %reduce-scatter.5.cloned.1.call-start = ((), (), s32[]{:S(2)}) async-start(), calls=%async_computation.4 | async-start | bytes 2359296 | tf_op jit(solution)/shard_map/reduce_scatter | solution.py:102
  107.9 11.5 %copy-start.5 = (f32[256,2048]{1,0:T(8,128)}, f32[256,2048]{1,0:T(8,128)S(1)}, u32[]{:S(2)}) copy-start(f32[256,2048]{1,0:T(8,128)S(1)} %fusion.34) | copy-start | bytes 6291460
  107.9 20.8 %copy-start.2 = (s32[2048]{0:T(1024)S(1)}, s32[2048]{0:T(1024)}, u32[]{:S(2)}) copy-start(s32[2048]{0:T(1024)} %param.11) | copy-start | bytes 24580
  108.0 22.1 %copy-start.1 = (f32[16,2048]{1,0:T(8,128)S(1)}, f32[16,2048]{1,0:T(8,128)}, u32[]{:S(2)}) copy-start(f32[16,2048]{1,0:T(8,128)} %param.8) | copy-start | bytes 393220
  109.2 1.6 collective-permute-start
  110.8 8.5 %collective-permute-start.1 = (f32[32,2048]{1,0:T(8,128)S(1)}, f32[32,2048]{1,0:T(8,128)S(1)}, u32[]{:S(2)}, u32[]{:S(2)}) collective-permute-start(f32[32,2048]{1,0:T(8,128)S(1)} %add.108), channel_id=1, source_target_pairs={{0,64},{64,0},{128,192},{192,128},{1,65},{65,1},{129,193},{193,129... | collective-permute-start | bytes 786440 | tf_op jit(solution)/shard_map/ppermute | solution.py:20
  119.4 9.2 %collective-permute-start.2 = (f32[32,2048]{1,0:T(8,128)S(1)}, f32[32,2048]{1,0:T(8,128)S(1)}, u32[]{:S(2)}, u32[]{:S(2)}) collective-permute-start(f32[32,2048]{1,0:T(8,128)S(1)} %add.109), channel_id=1, source_target_pairs={{0,128},{64,192},{128,0},{192,64},{1,129},{65,193},{129,1},{193,65... | collective-permute-start | bytes 786440 | tf_op jit(solution)/shard_map/ppermute | solution.py:20
  130.5 3.8 %collective-permute-start.3 = (f32[17,32]{1,0:T(8,128)S(1)}, f32[17,32]{1,0:T(8,128)S(1)}, u32[]{:S(2)}, u32[]{:S(2)}) collective-permute-start(f32[17,32]{1,0:T(8,128)S(1)} %pad_maximum_fusion), channel_id=1, source_target_pairs={{0,1},{1,0},{2,3},{3,2},{4,5},{5,4},{6,7},{7,6},{8,9},{9,8},{10,11... | collective-permute-start | bytes 6536 | tf_op jit(solution)/shard_map/ppermute | solution.py:20
  134.3 5.2 %collective-permute-start.4 = (f32[17,32]{1,0:T(8,128)S(1)}, f32[17,32]{1,0:T(8,128)S(1)}, u32[]{:S(2)}, u32[]{:S(2)}) collective-permute-start(f32[17,32]{1,0:T(8,128)S(1)} %fusion.32), channel_id=1, source_target_pairs={{0,2},{1,3},{2,0},{3,1},{4,6},{5,7},{6,4},{7,5},{8,10},{9,11},{10,... | collective-permute-start | bytes 6536 | tf_op jit(solution)/shard_map/ppermute | solution.py:20
  139.5 3.7 %collective-permute-start.5 = (f32[17,32]{1,0:T(8,128)S(1)}, f32[17,32]{1,0:T(8,128)S(1)}, u32[]{:S(2)}, u32[]{:S(2)}) collective-permute-start(f32[17,32]{1,0:T(8,128)S(1)} %add.114), channel_id=1, source_target_pairs={{0,4},{4,0},{8,12},{12,8},{16,20},{20,16},{24,28},{28,24},{1,5},{5... | collective-permute-start | bytes 6536 | tf_op jit(solution)/shard_map/ppermute | solution.py:20
  143.2 4.6 %collective-permute-start.6 = (f32[17,32]{1,0:T(8,128)S(1)}, f32[17,32]{1,0:T(8,128)S(1)}, u32[]{:S(2)}, u32[]{:S(2)}) collective-permute-start(f32[17,32]{1,0:T(8,128)S(1)} %add.115), channel_id=1, source_target_pairs={{0,8},{4,12},{8,0},{12,4},{16,24},{20,28},{24,16},{28,20},{1,9},{5... | collective-permute-start | bytes 6536 | tf_op jit(solution)/shard_map/ppermute | solution.py:20
  147.8 15.6 %collective-permute-start.7 = (f32[17,32]{1,0:T(8,128)S(1)}, f32[17,32]{1,0:T(8,128)S(1)}, u32[]{:S(2)}, u32[]{:S(2)}) collective-permute-start(f32[17,32]{1,0:T(8,128)S(1)} %add.116), channel_id=1, source_target_pairs={{0,16},{4,20},{8,24},{12,28},{16,0},{20,4},{24,8},{28,12},{1,17},{... | collective-permute-start | bytes 6536 | tf_op jit(solution)/shard_map/ppermute | solution.py:20
  153.5 9.9 %copy-start.4 = (s32[32]{0:T(128)S(1)}, s32[32]{0:T(128)}, u32[]{:S(2)}) copy-start(s32[32]{0:T(128)} %param.10) | copy-start | bytes 388
  153.5 10.4 %copy-start.6 = (f32[256,2048]{1,0:T(8,128)S(1)}, f32[256,2048]{1,0:T(8,128)}, u32[]{:S(2)}) copy-start(f32[256,2048]{1,0:T(8,128)} %copy-done.5) | copy-start | bytes 6291460
  165.6 1.0 copy-start.7
  170.2 83.1 %reduce-scatter.3.cloned.1.call-start = ((), (), s32[]{:S(2)}) async-start(), calls=%async_computation.3 | async-start | bytes 2359296 | tf_op jit(solution)/shard_map/reduce_scatter | solution.py:102
  210.2 45.9 %collective-permute-start.10 = (f32[128,256]{0,1:T(8,128)S(1)}, f32[128,256]{0,1:T(8,128)S(1)}, u32[]{:S(2)}, u32[]{:S(2)}) collective-permute-start(f32[128,256]{0,1:T(8,128)S(1)} %constant_dynamic-slice_fusion.1), channel_id=1, source_target_pairs={{0,2},{1,3},{2,0},{3,1},{4,6},{5,7},{6,4},{7,5},{8,10},{9,11},{10,... | collective-permute-start | bytes 393224 | tf_op jit(solution)/shard_map/ppermute | solution.py:33
  254.2 7.9 %collective-permute-start.8 = (f32[128,256]{0,1:T(8,128)S(1)}, f32[128,256]{0,1:T(8,128)S(1)}, u32[]{:S(2)}, u32[]{:S(2)}) collective-permute-start(f32[128,256]{0,1:T(8,128)S(1)} %constant_dynamic-slice_fusion.3), channel_id=1, source_target_pairs={{0,2},{1,3},{2,0},{3,1},{4,6},{5,7},{6,4},{7,5},{8,10},{9,11},{10,... | collective-permute-start | bytes 393224 | tf_op jit(solution)/shard_map/ppermute | solution.py:33
  257.1 6.1 %collective-permute-start.11 = (f32[64,256]{0,1:T(8,128)S(1)}, f32[64,256]{0,1:T(8,128)S(1)}, u32[]{:S(2)}, u32[]{:S(2)}) collective-permute-start(f32[64,256]{0,1:T(8,128)S(1)} %constant_dynamic-slice_fusion), channel_id=1, source_target_pairs={{0,1},{1,0},{2,3},{3,2},{4,5},{5,4},{6,7},{7,6},{8,9},{9,8},{10,11... | collective-permute-start | bytes 196616 | tf_op jit(solution)/shard_map/ppermute | solution.py:33
  263.2 5.1 %collective-permute-start.9 = (f32[64,256]{0,1:T(8,128)S(1)}, f32[64,256]{0,1:T(8,128)S(1)}, u32[]{:S(2)}, u32[]{:S(2)}) collective-permute-start(f32[64,256]{0,1:T(8,128)S(1)} %constant_dynamic-slice_fusion.2), channel_id=1, source_target_pairs={{0,1},{1,0},{2,3},{3,2},{4,5},{5,4},{6,7},{7,6},{8,9},{9,8},{10,11... | collective-permute-start | bytes 196616 | tf_op jit(solution)/shard_map/ppermute | solution.py:33
Sparse Core Ops, SparseCore 0:
  9.9 89.9 all-gather.1
  170.4 38.8 reduce-scatter.4
  211.8 41.4 reduce-scatter.2
where the time goes:
time: 276 us
  waiting for transfers between devices  197 us (71%)
  matrix products  22.8 us (8%)
  starting transfers between devices  21.3 us (8%)
  between operations  15.3 us (6%)
  local copies, waits for them, and re-layouts  13.5 us (5%)
  other arithmetic  5.73 us (2%)
    all_gather x1, waiting for transfers between devices, per_device(): full_head = lax.all_gather(head_weight, SEQ, axis=0, tiled=True)  91.5 us
    reduce_scatter x2, waiting for transfers between devices, per_device(): lax.psum_scatter(partial, 'vz', scatter_dimension=0, tiled=True)  69.4 us
    ppermute x8, waiting for transfers between devices, butterfly(): lax.ppermute(a, ax, [(i, i ^ d) for i in range(n)])  27.2 us
    ppermute x8, starting transfers between devices, butterfly(): lax.ppermute(a, ax, [(i, i ^ d) for i in range(n)])  15.2 us
    dot_general x2, matrix products, per_device(): lax.dot_general(rows, dlogits, (((1,), (1,)), ((), ())), preferred_elemen...  11.1 us
    slice x1, local copies, waits for them, and re-layouts, per_device(): rows = grouped[:, g].reshape(-1, vocab_cols)  9.88 us
    dot_general x1, matrix products, per_device(): logits = jnp.dot(hidden, full_head, preferred_element_type=jnp.float32)  8.11 us
    ppermute x4, waiting for transfers between devices, halving_scatter(): x = keep + lax.ppermute(send, ax, [(i, i ^ d) for i in range(n)])  7.99 us
  transfers between devices with their start and end apart: 15, of which 12 were waited for; matrix products, arithmetic and copies ran while one was open for 9% of the time, Pallas kernels for 0%

commit v1 on v0

--- a/solution.py
+++ b/solution.py
@@ -63,7 +63,9 @@
     counts = passage_lengths.astype(jnp.float32)
     weights_df = jnp.log(1.0 + DOCS / (1.0 + doc_freq.astype(jnp.float32)))
     flops_grad = loss_scale * flops_weight * 2.0 / (vocab_total * passages)
-    full_head = lax.all_gather(head_weight, SEQ, axis=0, tiled=True)
+    full_head = jnp.concatenate(
+        lax.all_to_all(jnp.stack([head_weight] * lax.axis_size(SEQ)), SEQ, 0, 0), axis=0
+    )
     logits = jnp.dot(hidden, full_head, preferred_element_type=jnp.float32)
     lifted = 1.0 + jax.nn.relu(logits)
     squared = lifted * lifted

time: 276 us -> 382 us (1.38)
  waiting for transfers between devices: 197 us -> 285 us
  starting transfers between devices: 21.3 us -> 31.7 us
  local copies, waits for them, and re-layouts: 13.5 us -> 20.6 us
    all_to_all x0 -> x1, waiting for transfers between devices: none -> 183 us  [per_device(): lax.all_to_all(jnp.stack([head_weight] * lax.axis_size(SEQ)), SEQ, 0, 0)]
    all_gather x1 -> x0, waiting for transfers between devices: 91.5 us -> none  [per_device(): full_head = lax.all_gather(head_weight, SEQ, axis=0, tiled=True)]
    another operation x1 -> x2, local copies, waits for them, and re-layouts: 0.09 us -> 7.14 us  [the longest x1 7.05 us: per_device(): jnp.stack([head_weight] * lax.axis_size(SEQ))]
    all_to_all x0 -> x1, starting transfers between devices: none -> 6.29 us  [per_device(): lax.all_to_all(jnp.stack([head_weight] * lax.axis_size(SEQ)), SEQ, 0, 0)]
    ppermute x8, starting transfers between devices: 15.2 us -> 19.3 us  [butterfly(): lax.ppermute(a, ax, [(i, i ^ d) for i in range(n)])]
  transfers between devices with their start and end apart: 15 -> 15, of which waited for: 12 -> 12; matrix products, arithmetic and copies ran while one was open for 9% -> 6% of each run, Pallas kernels for 0% -> 0%
where the time goes in v1:
time: 382 us
  waiting for transfers between devices  285 us (75%)
  starting transfers between devices  31.7 us (8%)
  matrix products  22.8 us (6%)
  local copies, waits for them, and re-layouts  20.6 us (5%)
  between operations  15.6 us (4%)
  other arithmetic  5.73 us (2%)
    all_to_all x1, waiting for transfers between devices, per_device(): lax.all_to_all(jnp.stack([head_weight] * lax.axis_size(SEQ)), SEQ, 0, 0)  183 us
    reduce_scatter x2, waiting for transfers between devices, per_device(): lax.psum_scatter(partial, 'vz', scatter_dimension=0, tiled=True)  69.9 us
    ppermute x8, waiting for transfers between devices, butterfly(): lax.ppermute(a, ax, [(i, i ^ d) for i in range(n)])  24.3 us
    ppermute x8, starting transfers between devices, butterfly(): lax.ppermute(a, ax, [(i, i ^ d) for i in range(n)])  19.3 us
    dot_general x2, matrix products, per_device(): lax.dot_general(rows, dlogits, (((1,), (1,)), ((), ())), preferred_elemen...  11.1 us
    slice x1, local copies, waits for them, and re-layouts, per_device(): rows = grouped[:, g].reshape(-1, vocab_cols)  9.89 us
    dot_general x1, matrix products, per_device(): logits = jnp.dot(hidden, full_head, preferred_element_type=jnp.float32)  8.11 us
    ppermute x4, waiting for transfers between devices, halving_scatter(): x = keep + lax.ppermute(send, ax, [(i, i ^ d) for i in range(n)])  8.08 us
  transfers between devices with their start and end apart: 15, of which 12 were waited for; matrix products, arithmetic and copies ran while one was open for 6% of the time, Pallas kernels for 0%

profile of v1, /device:TPU:10, one launch (start us, length us, event | category | flops | bytes accessed | tf_op | source)
XLA Modules:
  0.0 381.5 jit_solution(11102339219579797799)
XLA Ops:
  7.2 0.0 copy-start
  7.2 7.0 %stack.6 = bf16[8,512,2048]{2,1,0:T(8,128)(2,1)} broadcast(bf16[512,2048]{1,0:T(8,128)(2,1)} %param.7), dimensions={1,2} | broadcast | bytes 18874368 | tf_op jit(solution)/shard_map/stack | solution.py:67
  14.2 6.3 %all-to-all-start = ((bf16[8,512,2048]{2,1,0:T(8,128)(2,1)}), bf16[8,512,2048]{2,1,0:T(8,128)(2,1)}, u32[]{:S(2)}, u32[]{:S(2)}) async-start(bf16[8,512,2048]{2,1,0:T(8,128)(2,1)} %stack.6), calls=%async_computation | async-start | bytes 33554432 | tf_op jit(solution)/shard_map/all_to_all | solution.py:67
  20.5 0.0 reduce-scatter.3.cloned.1.call-start
  20.5 0.1 copy.9
  20.6 0.1 reduce-window.8
  20.7 0.1 reduce
  20.8 182.8 %all-to-all-done = bf16[8,512,2048]{2,1,0:T(8,128)(2,1)} async-done(((bf16[8,512,2048]{2,1,0:T(8,128)(2,1)}), bf16[8,512,2048]{2,1,0:T(8,128)(2,1)}, u32[]{:S(2)}, u32[]{:S(2)}) %all-to-all-start) | async-done | bytes 16777248 | tf_op jit(solution)/shard_map/all_to_all | solution.py:67
  203.7 8.1 %fusion.34 = f32[256,2048]{1,0:T(8,128)S(1)} fusion(bf16[256,4096]{1,0:T(8,128)(2,1)S(1)} %copy-done, bf16[4096,2048]{1,0:T(8,128)(2,1)} %bitcast), kind=kOutput, calls=%fused_computation.66 | convolution fusion | flops 4294967296 | bytes 20971520 | tf_op jit(solution)/shard_map/dot_general | solution.py:69
  211.8 0.0 copy-start.2
  211.8 0.0 copy-start.1
  211.8 1.2 fusion.3
  213.0 0.1 collective-permute-start
  213.1 1.5 collective-permute-done
  214.7 1.5 collective-permute-start.1
  216.2 6.9 %collective-permute-done.1 = f32[32,2048]{1,0:T(8,128)S(1)} collective-permute-done((f32[32,2048]{1,0:T(8,128)S(1)}, f32[32,2048]{1,0:T(8,128)S(1)}, u32[]{:S(2)}, u32[]{:S(2)}) %collective-permute-start.1) | collective-permute-done | bytes 262176 | tf_op jit(solution)/shard_map/ppermute | solution.py:20
  223.2 1.5 collective-permute-start.2
  224.7 7.6 %collective-permute-done.2 = f32[32,2048]{1,0:T(8,128)S(1)} collective-permute-done((f32[32,2048]{1,0:T(8,128)S(1)}, f32[32,2048]{1,0:T(8,128)S(1)}, u32[]{:S(2)}, u32[]{:S(2)}) %collective-permute-start.2) | collective-permute-done | bytes 262176 | tf_op jit(solution)/shard_map/ppermute | solution.py:20
  232.3 0.1 fusion.8
  232.4 0.6 fusion.17
  233.7 0.4 convolution_bitcast_fusion.2
  234.0 0.1 pad_maximum_fusion
  234.1 2.2 collective-permute-start.3
  236.3 1.7 collective-permute-done.3
  238.0 2.2 collective-permute-start.4
  240.2 3.0 collective-permute-done.4
  243.2 1.8 collective-permute-start.5
  245.0 1.9 collective-permute-done.5
  246.9 3.1 collective-permute-start.6
  250.1 1.7 collective-permute-done.6
  251.7 6.8 %collective-permute-start.7 = (f32[17,32]{1,0:T(8,128)S(1)}, f32[17,32]{1,0:T(8,128)S(1)}, u32[]{:S(2)}, u32[]{:S(2)}) collective-permute-start(f32[17,32]{1,0:T(8,128)S(1)} %add.116), channel_id=1, source_target_pairs={{0,16},{4,20},{8,24},{12,28},{16,0},{20,4},{24,8},{28,12},{1,17},{... | collective-permute-start | bytes 6536 | tf_op jit(solution)/shard_map/ppermute | solution.py:20
  258.6 9.9 %fusion.33 = (bf16[32,1,64,2048]{3,2,1,0:T(8,128)(2,1)S(1)}, bf16[32,1,64,2048]{3,2,1,0:T(8,128)(2,1)}) fusion(bf16[32,2,64,2048]{3,2,1,0:T(8,128)(2,1)} %bitcast.3), kind=kLoop, calls=%fused_computation.65 | loop fusion | bytes 33554432 | tf_op jit(solution)/shard_map/slice | solution.py:98
  268.5 0.0 collective-permute-done.7
  268.5 0.4 fusion.2
  269.0 0.0 copy-done.6
  269.0 1.6 fusion.1
  270.6 1.0 copy-done.7
  271.6 3.7 convolution_bitcast_fusion.1
  275.3 0.0 reduce-scatter.3.cloned.1.call-update
  275.3 0.0 reduce-scatter.5.cloned.1.call-start
  275.3 7.4 %convolution_bitcast_fusion = f32[2048,256]{0,1:T(8,128)} fusion(bf16[256,2048]{1,0:T(8,128)(2,1)} %copy-done.7, bf16[2048,2048]{1,0:T(8,128)(2,1)} %bitcast.24), kind=kOutput, calls=%fused_computation.2 | convolution fusion | flops 2147483648 | bytes 11534336 | tf_op jit(solution)/shard_map/dot_general | solution.py:99
  282.8 0.0 reduce-scatter.5.cloned.1.call-update
  282.8 0.5 slice.19
  283.4 0.6 subtract_reduce_fusion
  284.6 30.2 %reduce-scatter.3.cloned.1.call-done = f32[256,256]{0,1:T(8,128)} async-done(((f32[2048,256]{0,1:T(8,128)}), f32[256,256]{0,1:T(8,128)}) %reduce-scatter.3.cloned.1.call-update) | async-done | bytes 262160 | tf_op jit(solution)/shard_map/reduce_scatter | solution.py:104
  314.8 0.9 constant_dynamic-slice_fusion.3
  315.8 2.2 collective-permute-start.8
  318.0 1.2 pad_maximum_fusion.1
  319.2 39.7 %reduce-scatter.5.cloned.1.call-done = f32[256,256]{0,1:T(8,128)} async-done(((f32[2048,256]{0,1:T(8,128)}), f32[256,256]{0,1:T(8,128)}) %reduce-scatter.5.cloned.1.call-update) | async-done | bytes 262160 | tf_op jit(solution)/shard_map/reduce_scatter | solution.py:104
  358.9 0.9 constant_dynamic-slice_fusion.1
  359.8 2.2 collective-permute-start.10
  362.0 0.0 collective-permute-done.8
  362.0 0.9 dynamic-slice_add_fusion.1
  362.9 0.1 constant_dynamic-slice_fusion.2
  363.0 1.5 collective-permute-start.9
  364.5 3.2 collective-permute-done.10
  367.8 0.9 dynamic-slice_add_fusion
  368.7 0.1 constant_dynamic-slice_fusion
  368.8 0.1 collective-permute-start.11
  368.9 0.0 collective-permute-done.9
  368.9 0.1 add_convert_fusion.1
  369.0 4.8 %collective-permute-done.11 = f32[64,256]{0,1:T(8,128)S(1)} collective-permute-done((f32[64,256]{0,1:T(8,128)S(1)}, f32[64,256]{0,1:T(8,128)S(1)}, u32[]{:S(2)}, u32[]{:S(2)}) %collective-permute-start.11) | collective-permute-done | bytes 65568 | tf_op jit(solution)/shard_map/ppermute | solution.py:33
  373.9 0.1 add_convert_fusion
  374.0 0.7 maximum_bitcast_fusion
  (24 shorter events, 0.2 us)
Async XLA Ops:
  7.2 196.5 %copy-start = (bf16[256,4096]{1,0:T(8,128)(2,1)S(1)}, bf16[256,4096]{1,0:T(8,128)(2,1)}, u32[]{:S(2)}) copy-start(bf16[256,4096]{1,0:T(8,128)(2,1)} %param.6) | copy-start | bytes 6291460
  14.2 6.3 %copy-start.3 = (s32[32]{0:T(128)S(1)}, s32[32]{0:T(128)}, u32[]{:S(2)}) copy-start(s32[32]{0:T(128)} %param.9) | copy-start | bytes 388
  14.2 189.4 %all-to-all-start = ((bf16[8,512,2048]{2,1,0:T(8,128)(2,1)}), bf16[8,512,2048]{2,1,0:T(8,128)(2,1)}, u32[]{:S(2)}, u32[]{:S(2)}) async-start(bf16[8,512,2048]{2,1,0:T(8,128)(2,1)} %stack.6), calls=%async_computation | async-start | bytes 33554432 | tf_op jit(solution)/shard_map/all_to_all | solution.py:67
  20.5 294.3 %reduce-scatter.3.cloned.1.call-start = ((), (), s32[]{:S(2)}) async-start(), calls=%async_computation.3 | async-start | bytes 2359296 | tf_op jit(solution)/shard_map/reduce_scatter | solution.py:104
  211.8 11.4 %copy-start.5 = (f32[256,2048]{1,0:T(8,128)}, f32[256,2048]{1,0:T(8,128)S(1)}, u32[]{:S(2)}) copy-start(f32[256,2048]{1,0:T(8,128)S(1)} %fusion.34) | copy-start | bytes 6291460
  211.8 20.6 %copy-start.2 = (s32[2048]{0:T(1024)S(1)}, s32[2048]{0:T(1024)}, u32[]{:S(2)}) copy-start(s32[2048]{0:T(1024)} %param.11) | copy-start | bytes 24580
  211.8 21.9 %copy-start.1 = (f32[16,2048]{1,0:T(8,128)S(1)}, f32[16,2048]{1,0:T(8,128)}, u32[]{:S(2)}) copy-start(f32[16,2048]{1,0:T(8,128)} %param.8) | copy-start | bytes 393220
  213.0 1.6 collective-permute-start
  214.7 8.4 %collective-permute-start.1 = (f32[32,2048]{1,0:T(8,128)S(1)}, f32[32,2048]{1,0:T(8,128)S(1)}, u32[]{:S(2)}, u32[]{:S(2)}) collective-permute-start(f32[32,2048]{1,0:T(8,128)S(1)} %add.108), channel_id=1, source_target_pairs={{0,64},{64,0},{128,192},{192,128},{1,65},{65,1},{129,193},{193,129... | collective-permute-start | bytes 786440 | tf_op jit(solution)/shard_map/ppermute | solution.py:20
  223.2 9.1 %collective-permute-start.2 = (f32[32,2048]{1,0:T(8,128)S(1)}, f32[32,2048]{1,0:T(8,128)S(1)}, u32[]{:S(2)}, u32[]{:S(2)}) collective-permute-start(f32[32,2048]{1,0:T(8,128)S(1)} %add.109), channel_id=1, source_target_pairs={{0,128},{64,192},{128,0},{192,64},{1,129},{65,193},{129,1},{193,65... | collective-permute-start | bytes 786440 | tf_op jit(solution)/shard_map/ppermute | solution.py:20
  234.1 3.9 %collective-permute-start.3 = (f32[17,32]{1,0:T(8,128)S(1)}, f32[17,32]{1,0:T(8,128)S(1)}, u32[]{:S(2)}, u32[]{:S(2)}) collective-permute-start(f32[17,32]{1,0:T(8,128)S(1)} %pad_maximum_fusion), channel_id=1, source_target_pairs={{0,1},{1,0},{2,3},{3,2},{4,5},{5,4},{6,7},{7,6},{8,9},{9,8},{10,11... | collective-permute-start | bytes 6536 | tf_op jit(solution)/shard_map/ppermute | solution.py:20
  238.0 5.2 %collective-permute-start.4 = (f32[17,32]{1,0:T(8,128)S(1)}, f32[17,32]{1,0:T(8,128)S(1)}, u32[]{:S(2)}, u32[]{:S(2)}) collective-permute-start(f32[17,32]{1,0:T(8,128)S(1)} %fusion.32), channel_id=1, source_target_pairs={{0,2},{1,3},{2,0},{3,1},{4,6},{5,7},{6,4},{7,5},{8,10},{9,11},{10,... | collective-permute-start | bytes 6536 | tf_op jit(solution)/shard_map/ppermute | solution.py:20
  243.2 3.7 collective-permute-start.5
  246.9 4.8 %collective-permute-start.6 = (f32[17,32]{1,0:T(8,128)S(1)}, f32[17,32]{1,0:T(8,128)S(1)}, u32[]{:S(2)}, u32[]{:S(2)}) collective-permute-start(f32[17,32]{1,0:T(8,128)S(1)} %add.115), channel_id=1, source_target_pairs={{0,8},{4,12},{8,0},{12,4},{16,24},{20,28},{24,16},{28,20},{1,9},{5... | collective-permute-start | bytes 6536 | tf_op jit(solution)/shard_map/ppermute | solution.py:20
  251.7 16.7 %collective-permute-start.7 = (f32[17,32]{1,0:T(8,128)S(1)}, f32[17,32]{1,0:T(8,128)S(1)}, u32[]{:S(2)}, u32[]{:S(2)}) collective-permute-start(f32[17,32]{1,0:T(8,128)S(1)} %add.116), channel_id=1, source_target_pairs={{0,16},{4,20},{8,24},{12,28},{16,0},{20,4},{24,8},{28,12},{1,17},{... | collective-permute-start | bytes 6536 | tf_op jit(solution)/shard_map/ppermute | solution.py:20
  258.6 9.9 %copy-start.4 = (s32[32]{0:T(128)S(1)}, s32[32]{0:T(128)}, u32[]{:S(2)}) copy-start(s32[32]{0:T(128)} %param.10) | copy-start | bytes 388
  258.6 10.4 %copy-start.6 = (f32[256,2048]{1,0:T(8,128)S(1)}, f32[256,2048]{1,0:T(8,128)}, u32[]{:S(2)}) copy-start(f32[256,2048]{1,0:T(8,128)} %copy-done.5) | copy-start | bytes 6291460
  270.6 1.0 copy-start.7
  275.3 83.6 %reduce-scatter.5.cloned.1.call-start = ((), (), s32[]{:S(2)}) async-start(), calls=%async_computation.4 | async-start | bytes 2359296 | tf_op jit(solution)/shard_map/reduce_scatter | solution.py:104
  315.8 46.3 %collective-permute-start.8 = (f32[128,256]{0,1:T(8,128)S(1)}, f32[128,256]{0,1:T(8,128)S(1)}, u32[]{:S(2)}, u32[]{:S(2)}) collective-permute-start(f32[128,256]{0,1:T(8,128)S(1)} %constant_dynamic-slice_fusion.3), channel_id=1, source_target_pairs={{0,2},{1,3},{2,0},{3,1},{4,6},{5,7},{6,4},{7,5},{8,10},{9,11},{10,... | collective-permute-start | bytes 393224 | tf_op jit(solution)/shard_map/ppermute | solution.py:33
  359.8 7.9 %collective-permute-start.10 = (f32[128,256]{0,1:T(8,128)S(1)}, f32[128,256]{0,1:T(8,128)S(1)}, u32[]{:S(2)}, u32[]{:S(2)}) collective-permute-start(f32[128,256]{0,1:T(8,128)S(1)} %constant_dynamic-slice_fusion.1), channel_id=1, source_target_pairs={{0,2},{1,3},{2,0},{3,1},{4,6},{5,7},{6,4},{7,5},{8,10},{9,11},{10,... | collective-permute-start | bytes 393224 | tf_op jit(solution)/shard_map/ppermute | solution.py:33
  363.0 5.9 %collective-permute-start.9 = (f32[64,256]{0,1:T(8,128)S(1)}, f32[64,256]{0,1:T(8,128)S(1)}, u32[]{:S(2)}, u32[]{:S(2)}) collective-permute-start(f32[64,256]{0,1:T(8,128)S(1)} %constant_dynamic-slice_fusion.2), channel_id=1, source_target_pairs={{0,1},{1,0},{2,3},{3,2},{4,5},{5,4},{6,7},{7,6},{8,9},{9,8},{10,11... | collective-permute-start | bytes 196616 | tf_op jit(solution)/shard_map/ppermute | solution.py:33
  368.8 5.1 %collective-permute-start.11 = (f32[64,256]{0,1:T(8,128)S(1)}, f32[64,256]{0,1:T(8,128)S(1)}, u32[]{:S(2)}, u32[]{:S(2)}) collective-permute-start(f32[64,256]{0,1:T(8,128)S(1)} %constant_dynamic-slice_fusion), channel_id=1, source_target_pairs={{0,1},{1,0},{2,3},{3,2},{4,5},{5,4},{6,7},{7,6},{8,9},{9,8},{10,11... | collective-permute-start | bytes 196616 | tf_op jit(solution)/shard_map/ppermute | solution.py:33
Sparse Core Ops, SparseCore 0:
  275.4 39.3 reduce-scatter.2
  317.4 41.4 reduce-scatter.4
